TPU v7x, 256 devices: a whole 4x4x8 slice. The times are simulated.
256 devices in a mesh: gx: 32 (over z_hi, y, core), gy: 8 (over x, z_lo).
Axes of the slice: x: 4, y: 4, z: 8 (z_hi: 4, z_lo: 2; z = z_hi * 2 + z_lo), core: 2. Of those that a mesh axis runs over, the one named last changes fastest.
Arguments:
- kernel: bfloat16 [262144, 512], P(('gx', 'gy')), may hold values from -0.25 to 0.25
- margin: bfloat16 [262144, 512], P(('gx', 'gy')), may hold values from -0.25 to 0.25
- hamiltonian: bfloat16 [262144, 512], P(('gx', 'gy')), may hold values from -9 to 9
- columns: int32 [4096, 8], replicated, may hold values from -1 to 4095, as said below
Outputs:
- gradient_term: float32 [262144, 512], P(('gx', 'gy'))
Inputs may be any that keep to these rules, and one draw needn't show every extreme that they name: `columns`: clusters are numbered device by device, 16 each, device number = gx index * (devices along gy) + gy index. Slot 0 of row i names i itself; the live ids of a row are distinct, live slots come first and the rest hold -1; every device has a row with all 8 slots live. A row of the device at (x, y) names only clusters of its own device and clusters number r + 4 * (2 p + q) (r < 4, counted within the device) of the device at (x + s, y + t), indices wrapping around, with s and t in -1, 0, 1, where p = 1 if s = -1, p = 0 if s = 1, either if s = 0, and likewise q from t.
All inputs are finite; a program needn't handle non-finite values.
Results may differ from a plain program's by a relative error of at most 0.005.
Values may be sent and summed in bfloat16 or wider, within the bound.
No kernel may reach another device: no remote copies, remote signals or barrier semaphores. Data moves between devices by JAX's collectives and lax.ppermute only.
A program may use at most 128 MiB of HBM per device.

v0:
```python
import math

import jax
import jax.numpy as jnp
from jax import lax
from jax.sharding import PartitionSpec as P

BS = 64
NB = 8
EDGE = 4
BLK_DEV = 16


def extended_2(cells, sides, width):
    for axis, dim in sides:
        count = lax.axis_size(axis)
        head = lax.slice_in_dim(cells, 0, width, axis=dim)
        tail = lax.slice_in_dim(cells, cells.shape[dim] - width, cells.shape[dim], axis=dim)
        cells = jnp.concatenate(
            [
                lax.ppermute(tail, axis, [(i, (i + 1) % count) for i in range(count)]),
                cells,
                lax.ppermute(head, axis, [((i + 1) % count, i) for i in range(count)]),
            ],
            axis=dim,
        )
    return cells


def outgoing(matrix):
    return matrix.reshape(2, 2, EDGE * BS, NB * BS)


def row_layout(local, received):
    far_rows = received.reshape(-1, NB * BS)
    joined = jnp.concatenate([local, far_rows], axis=0)
    return joined.reshape(-1, BS, NB * BS)


def pattern_product(left, extended, position, mapping):
    row_count = left.shape[0] // BS
    group = math.gcd(row_count, 4)
    lefts = left.reshape(row_count // group, group, BS, NB, BS)
    places = position.reshape(row_count // group, group, NB)
    maps = mapping.reshape(row_count // group, group, NB, NB, NB)

    def product_rows(pieces):
        left_rows, place_rows, map_rows = pieces
        far_rows = extended[place_rows].reshape(group, NB, BS, NB, BS)
        moved = jnp.einsum(
            "iasct,iacb->iasbt", far_rows, map_rows, preferred_element_type=jnp.float32
        ).astype(jnp.bfloat16)
        return jnp.einsum("iras,iasbt->irbt", left_rows, moved, preferred_element_type=jnp.float32)

    result = lax.map(product_rows, (lefts, places, maps))
    return result.reshape(left.shape[0], NB * BS)


def body(kernel, margin, hamiltonian, columns):
    block_count = BLK_DEV
    gx_index = lax.axis_index("gx")
    gy_index = lax.axis_index("gy")
    along_gy = lax.axis_size("gy")
    first_block = (gx_index * along_gy + gy_index) * block_count
    own_columns = lax.dynamic_slice_in_dim(columns, first_block, block_count, 0)
    offsets = jnp.array([-1, 0, 0, 1], jnp.int32)
    corner_side = jnp.array([1, 0, 1, 0], jnp.int32)
    source_x = (gx_index + offsets) % lax.axis_size("gx")
    source_y = (gy_index + offsets) % along_gy
    owners = source_x[:, None] * along_gy + source_y[None, :]
    quadrant = (2 * corner_side[:, None] + corner_side[None, :]) * EDGE
    ghost_ids = (
        owners[:, :, None] * block_count
        + quadrant[:, :, None]
        + jnp.arange(EDGE, dtype=jnp.int32)[None, None, :]
    ).reshape(-1)
    extended_ids = jnp.concatenate(
        [first_block + jnp.arange(block_count, dtype=jnp.int32), ghost_ids]
    )
    extended_count = extended_ids.shape[0]
    extended_columns = columns[extended_ids]
    is_live = own_columns >= 0
    found = extended_ids[None, None, :] == own_columns[:, :, None]
    position = jnp.min(
        jnp.where(
            found, jnp.arange(extended_count, dtype=jnp.int32)[None, None, :], extended_count
        ),
        axis=2,
    )
    position = jnp.where(is_live, position, 0)
    far_columns = extended_columns[position]
    matched = (
        (far_columns[:, :, :, None] == own_columns[:, None, None, :])
        & is_live[:, :, None, None]
        & is_live[:, None, None, :]
    )
    mapping = matched.astype(jnp.bfloat16)
    both = jnp.stack([outgoing(kernel), outgoing(margin)], axis=2)
    arrived = extended_2(both, (("gx", 0), ("gy", 1)), 1)
    kernel_ext = row_layout(kernel, arrived[:, :, 0])
    margin_ext = row_layout(margin, arrived[:, :, 1])
    lead_product = pattern_product(kernel, margin_ext, position, mapping).astype(jnp.bfloat16)
    cubic = pattern_product(lead_product, kernel_ext, position, mapping).astype(jnp.bfloat16)
    cubic_arrived = extended_2(outgoing(cubic), (("gx", 0), ("gy", 1)), 1)
    fifth = pattern_product(lead_product, row_layout(cubic, cubic_arrived), position, mapping)
    purified = (3.0 * cubic.astype(jnp.float32) - 2.0 * fifth).astype(jnp.bfloat16)
    purified_arrived = extended_2(outgoing(purified), (("gx", 0), ("gy", 1)), 1)
    return pattern_product(hamiltonian, row_layout(purified, purified_arrived), position, mapping)


def solution(mesh):
    in_specs = (P(("gx", "gy"), None), P(("gx", "gy"), None), P(("gx", "gy"), None), P())
    out_specs = P(("gx", "gy"), None)
    return jax.shard_map(body, mesh=mesh, in_specs=in_specs, out_specs=out_specs, check_vma=False)
```

profile of v0, /device:TPU:2, one launch (start us, length us, event | category | flops | bytes accessed | tf_op | source)
XLA Modules:
  0.0 525.0 jit_solution(3376168479702953844)
XLA Ops:
  1.9 8.3 %collective-permute-start.1 = (bf16[1,2,2,256,512]{4,3,1,0,2:T(8,128)(2,1)S(1)}, bf16[1,2,2,256,512]{4,3,1,0,2:T(8,128)(2,1)S(1)}, u32[]{:S(2)}, u32[]{:S(2)}) collective-permute-start(bf16[1,2,2,256,512]{4,3,1,0,2:T(8,128)(2,1)S(1)} %get-tuple-element.225), channel_id=1, source_target_pairs={{8,0},{16,8},{24,16},{32,24},{40,32},{48,40},{56,48},{64,56},{72,6... | collective-permute-start | bytes 3145736 | tf_op jit(solution)/shard_map/ppermute | solution.py:23
  10.2 16.7 %collective-permute-done = bf16[1,2,2,256,512]{4,3,1,0,2:T(8,128)(2,1)S(1)} collective-permute-done((bf16[1,2,2,256,512]{4,3,1,0,2:T(8,128)(2,1)S(1)}, bf16[1,2,2,256,512]{4,3,1,0,2:T(8,128)(2,1)S(1)}, u32[]{:S(2)}, u32[]{:S(2)}) %collective-permute-start) | collective-permute-done | bytes 1048608 | tf_op jit(solution)/shard_map/ppermute | solution.py:21
  27.0 6.5 %collective-permute-done.1 = bf16[1,2,2,256,512]{4,3,1,0,2:T(8,128)(2,1)S(1)} collective-permute-done((bf16[1,2,2,256,512]{4,3,1,0,2:T(8,128)(2,1)S(1)}, bf16[1,2,2,256,512]{4,3,1,0,2:T(8,128)(2,1)S(1)}, u32[]{:S(2)}, u32[]{:S(2)}) %collective-permute-start.1) | collective-permute-done | bytes 1048608 | tf_op jit(solution)/shard_map/ppermute | solution.py:23
  53.3 33.8 %collective-permute-done.2 = bf16[4,1,2,256,512]{4,3,1,0,2:T(8,128)(2,1)} collective-permute-done((bf16[4,1,2,256,512]{4,3,1,0,2:T(8,128)(2,1)}, bf16[4,1,2,256,512]{4,3,1,0,2:T(8,128)(2,1)}, u32[]{:S(2)}, u32[]{:S(2)}) %collective-permute-start.2) | collective-permute-done | bytes 2097184 | tf_op jit(solution)/shard_map/ppermute | solution.py:21
  87.1 36.9 %collective-permute-done.3 = bf16[4,1,2,256,512]{4,3,1,0,2:T(8,128)(2,1)} collective-permute-done((bf16[4,1,2,256,512]{4,3,1,0,2:T(8,128)(2,1)}, bf16[4,1,2,256,512]{4,3,1,0,2:T(8,128)(2,1)}, u32[]{:S(2)}, u32[]{:S(2)}) %collective-permute-start.3) | collective-permute-done | bytes 2097184 | tf_op jit(solution)/shard_map/ppermute | solution.py:23
  124.0 3.9 pad_maximum_fusion
  133.0 55.3 %while.44 = (s32[]{:T(128)}, bf16[4,4,64,8,64]{4,2,3,1,0:T(8,128)(2,1)}, bf16[4,4,64,8,64]{4,3,2,1,0:T(8,128)(2,1)}, bf16[4,4,8,8,8]{3,4,2,1,0:T(8,128)(2,1)S(1)...) while((s32[]{:T(128)}, bf16[4,4,64,8,64]{4,2,3,1,0:T(8,128)(2,1)}, ...), condition=%wide.region_2.3_spmd.clone, body=%wide.region_1.2_spmd.sunk.clone | while | flops 152044640 | bytes 27333516 | solution.py:55
  133.1 3.2 gather_fusion
  136.3 3.6 reshape.455
  139.9 3.6 convert_bitcast_fusion.12
  146.9 3.2 gather_fusion
  150.1 3.6 reshape.455
  153.7 3.6 convert_bitcast_fusion.12
  160.8 3.2 gather_fusion
  163.9 3.6 reshape.455
  167.5 3.6 convert_bitcast_fusion.12
  174.6 3.2 gather_fusion
  177.8 3.6 reshape.455
  181.4 3.6 convert_bitcast_fusion.12
  188.3 4.8 pad_maximum_fusion.2
  193.2 55.2 %while.45 = (s32[]{:T(128)}, bf16[4,4,64,8,64]{4,2,3,1,0:T(8,128)(2,1)}, bf16[4,4,64,8,64]{4,2,3,1,0:T(8,128)(2,1)}, bf16[4,4,8,8,8]{3,4,2,1,0:T(8,128)(2,1)S(1)...) while((s32[]{:T(128)}, bf16[4,4,64,8,64]{4,2,3,1,0:T(8,128)(2,1)}, ...), condition=%wide.region_4.5_spmd.clone, body=%wide.region_3.4_spmd.sunk.clone | while | flops 152044640 | bytes 26810244 | solution.py:55
  193.3 3.2 gather_fusion.1
  196.4 3.6 reshape.459
  200.0 3.6 convert_bitcast_fusion.13
  207.0 3.2 gather_fusion.1
  210.2 3.6 reshape.459
  213.8 3.6 convert_bitcast_fusion.13
  220.8 3.2 gather_fusion.1
  224.0 3.6 reshape.459
  227.6 3.6 convert_bitcast_fusion.13
  237.8 3.6 reshape.459
  241.4 3.6 convert_bitcast_fusion.13
  257.0 5.9 %collective-permute-start.5 = (bf16[1,2,256,512]{3,2,1,0:T(8,128)(2,1)}, bf16[1,2,256,512]{3,2,1,0:T(8,128)(2,1)}, u32[]{:S(2)}, u32[]{:S(2)}) collective-permute-start(bf16[1,2,256,512]{3,2,1,0:T(8,128)(2,1)} %slice.65), channel_id=1, source_target_pairs={{8,0},{16,8},{24,16},{32,24},{40,32},{48,40},{56,48},{64,56},{72,6... | collective-permute-start | bytes 1572872 | tf_op jit(solution)/shard_map/ppermute | solution.py:23
  266.0 3.2 convert_element_type.60
  282.9 22.9 %collective-permute-done.6 = bf16[4,1,256,512]{3,2,1,0:T(8,128)(2,1)} collective-permute-done((bf16[4,1,256,512]{3,2,1,0:T(8,128)(2,1)}, bf16[4,1,256,512]{3,2,1,0:T(8,128)(2,1)}, u32[]{:S(2)}, u32[]{:S(2)}) %collective-permute-start.6) | collective-permute-done | bytes 1048608 | tf_op jit(solution)/shard_map/ppermute | solution.py:21
  305.8 15.6 %collective-permute-done.7 = bf16[4,1,256,512]{3,2,1,0:T(8,128)(2,1)} collective-permute-done((bf16[4,1,256,512]{3,2,1,0:T(8,128)(2,1)}, bf16[4,1,256,512]{3,2,1,0:T(8,128)(2,1)}, u32[]{:S(2)}, u32[]{:S(2)}) %collective-permute-start.7) | collective-permute-done | bytes 1048608 | tf_op jit(solution)/shard_map/ppermute | solution.py:23
  326.4 53.0 %while.46 = (s32[]{:T(128)}, f32[4,4,64,8,64]{4,2,3,1,0:T(8,128)}, bf16[4,4,64,8,64]{4,2,3,1,0:T(8,128)(2,1)}, bf16[4,4,8,8,8]{3,4,2,1,0:T(8,128)(2,1)S(1)}, s32...) while((s32[]{:T(128)}, f32[4,4,64,8,64]{4,2,3,1,0:T(8,128)}, ...), condition=%wide.region_6.7_spmd.clone, body=%wide.region_5.6_spmd.sunk.clone | while | flops 152044640 | bytes 16324429 | solution.py:55
  329.7 3.6 reshape.463
  333.3 3.4 convert_bitcast_fusion.14
  342.9 3.6 reshape.463
  346.5 3.4 convert_bitcast_fusion.14
  353.0 3.2 gather_fusion.2
  356.2 3.6 reshape.463
  359.8 3.4 convert_bitcast_fusion.14
  369.5 3.6 reshape.463
  373.1 3.4 convert_bitcast_fusion.14
  382.0 5.3 %copy.32 = f32[4,4,64,8,64]{4,3,2,1,0:T(8,128)} copy(f32[4,4,64,8,64]{4,2,3,1,0:T(8,128)S(1)} %broadcast_multiply_fusion) | data formatting | bytes 4194304 | tf_op jit(solution)/shard_map/mul | solution.py:106
  387.3 4.8 mul.63
  395.1 6.2 %collective-permute-start.9 = (bf16[1,2,256,512]{3,2,1,0:T(8,128)(2,1)}, bf16[1,2,256,512]{3,2,1,0:T(8,128)(2,1)}, u32[]{:S(2)}, u32[]{:S(2)}) collective-permute-start(bf16[1,2,256,512]{3,2,1,0:T(8,128)(2,1)} %bitcast.59), channel_id=1, source_target_pairs={{8,0},{16,8},{24,16},{32,24},{40,32},{48,40},{56,48},{64,56},{72,6... | collective-permute-start | bytes 1572872 | tf_op jit(solution)/shard_map/ppermute | solution.py:23
  401.3 4.8 mul.66
  408.0 9.1 %collective-permute-done.8 = bf16[1,2,256,512]{3,2,1,0:T(8,128)(2,1)} collective-permute-done((bf16[1,2,256,512]{3,2,1,0:T(8,128)(2,1)}, bf16[1,2,256,512]{3,2,1,0:T(8,128)(2,1)}, u32[]{:S(2)}, u32[]{:S(2)}) %collective-permute-start.8) | collective-permute-done | bytes 524320 | tf_op jit(solution)/shard_map/ppermute | solution.py:21
  425.0 22.3 %collective-permute-done.10 = bf16[4,1,256,512]{3,2,1,0:T(8,128)(2,1)} collective-permute-done((bf16[4,1,256,512]{3,2,1,0:T(8,128)(2,1)}, bf16[4,1,256,512]{3,2,1,0:T(8,128)(2,1)}, u32[]{:S(2)}, u32[]{:S(2)}) %collective-permute-start.10) | collective-permute-done | bytes 1048608 | tf_op jit(solution)/shard_map/ppermute | solution.py:21
  447.3 12.3 %collective-permute-done.11 = bf16[4,1,256,512]{3,2,1,0:T(8,128)(2,1)} collective-permute-done((bf16[4,1,256,512]{3,2,1,0:T(8,128)(2,1)}, bf16[4,1,256,512]{3,2,1,0:T(8,128)(2,1)}, u32[]{:S(2)}, u32[]{:S(2)}) %collective-permute-start.11) | collective-permute-done | bytes 1048608 | tf_op jit(solution)/shard_map/ppermute | solution.py:23
  464.4 55.6 %while.47 = (s32[]{:T(128)}, f32[4,4,64,8,64]{4,3,2,1,0:T(8,128)}, bf16[4,4,64,8,64]{4,3,2,1,0:T(8,128)(2,1)}, bf16[4,4,8,8,8]{3,4,2,1,0:T(8,128)(2,1)S(1)}, s32...) while((s32[]{:T(128)}, f32[4,4,64,8,64]{4,3,2,1,0:T(8,128)}, ...), condition=%wide.region_8.9_spmd.clone, body=%wide.region_7.8_spmd.sunk.clone | while | flops 152044640 | bytes 17634640 | solution.py:55
  467.7 3.6 reshape.467
  471.3 3.4 convert_bitcast_fusion.15
  481.6 3.6 reshape.467
  485.2 3.4 convert_bitcast_fusion.15
  492.2 3.2 gather_fusion.3
  495.4 3.6 reshape.467
  499.0 3.4 convert_bitcast_fusion.15
  509.4 3.6 reshape.467
  513.0 3.4 convert_bitcast_fusion.15
  520.0 4.8 reshape.348
  (207 shorter events, 153.9 us)
Async XLA Ops:
  0.0 34.5 %copy-start.4 = (bf16[1024,512]{1,0:T(8,128)(2,1)S(1)}, bf16[1024,512]{1,0:T(8,128)(2,1)}, u32[]{:S(2)}) copy-start(bf16[1024,512]{1,0:T(8,128)(2,1)} %param.14) | copy-start | bytes 3145732
  0.0 34.5 %copy-start.6 = (bf16[1024,512]{1,0:T(8,128)(2,1)S(1)}, bf16[1024,512]{1,0:T(8,128)(2,1)}, u32[]{:S(2)}) copy-start(bf16[1024,512]{1,0:T(8,128)(2,1)} %param.15) | copy-start | bytes 3145732
  1.9 25.1 %collective-permute-start = (bf16[1,2,2,256,512]{4,3,1,0,2:T(8,128)(2,1)S(1)}, bf16[1,2,2,256,512]{4,3,1,0,2:T(8,128)(2,1)S(1)}, u32[]{:S(2)}, u32[]{:S(2)}) collective-permute-start(bf16[1,2,2,256,512]{4,3,1,0,2:T(8,128)(2,1)S(1)} %get-tuple-element.224), channel_id=1, source_target_pairs={{0,8},{8,16},{16,24},{24,32},{32,40},{40,48},{48,56},{56,64},{64,7... | collective-permute-start | bytes 3145736 | tf_op jit(solution)/shard_map/ppermute | solution.py:21
  1.9 31.6 %collective-permute-start.1 = (bf16[1,2,2,256,512]{4,3,1,0,2:T(8,128)(2,1)S(1)}, bf16[1,2,2,256,512]{4,3,1,0,2:T(8,128)(2,1)S(1)}, u32[]{:S(2)}, u32[]{:S(2)}) collective-permute-start(bf16[1,2,2,256,512]{4,3,1,0,2:T(8,128)(2,1)S(1)} %get-tuple-element.225), channel_id=1, source_target_pairs={{8,0},{16,8},{24,16},{32,24},{40,32},{48,40},{56,48},{64,56},{72,6... | collective-permute-start | bytes 3145736 | tf_op jit(solution)/shard_map/ppermute | solution.py:23
  27.0 10.4 %copy-start.10 = (bf16[1,2,2,256,512]{4,3,1,0,2:T(8,128)(2,1)}, bf16[1,2,2,256,512]{4,3,1,0,2:T(8,128)(2,1)S(1)}, u32[]{:S(2)}) copy-start(bf16[1,2,2,256,512]{4,3,1,0,2:T(8,128)(2,1)S(1)} %collective-permute-done) | copy-start | bytes 3145732
  33.5 1.0 copy-start.11
  35.0 5.6 %copy-start.16 = (s32[4]{0:T(128)S(1)}, s32[4]{0:T(128)}, u32[]{:S(2)}) copy-start(s32[4]{0:T(128)} %constant.116.clone) | copy-start | bytes 52
  35.1 5.6 %copy-start.17 = (s32[4]{0:T(128)S(1)}, s32[4]{0:T(128)}, u32[]{:S(2)}) copy-start(s32[4]{0:T(128)} %constant.117.clone) | copy-start | bytes 52
  35.1 5.6 %copy-start.18 = (s32[4]{0:T(128)S(1)}, s32[4]{0:T(128)}, u32[]{:S(2)}) copy-start(s32[4]{0:T(128)} %constant.118) | copy-start | bytes 52
  35.1 8.0 %copy-start.15 = (s32[4096,8]{0,1:T(8,128)S(1)}, s32[4096,8]{0,1:T(8,128)}, u32[]{:S(2)}) copy-start(s32[4096,8]{0,1:T(8,128)} %param.17) | copy-start | bytes 393220
  37.4 49.7 %collective-permute-start.2 = (bf16[4,1,2,256,512]{4,3,1,0,2:T(8,128)(2,1)}, bf16[4,1,2,256,512]{4,3,1,0,2:T(8,128)(2,1)}, u32[]{:S(2)}, u32[]{:S(2)}) collective-permute-start(bf16[4,1,2,256,512]{4,3,1,0,2:T(8,128)(2,1)} %get-tuple-element.216), channel_id=1, source_target_pairs={{0,1},{1,2},{2,3},{3,4},{4,5},{5,6},{6,7},{7,0},{8,9},{9,10},{10,1... | collective-permute-start | bytes 6291464 | tf_op jit(solution)/shard_map/ppermute | solution.py:21
  38.9 85.1 %collective-permute-start.3 = (bf16[4,1,2,256,512]{4,3,1,0,2:T(8,128)(2,1)}, bf16[4,1,2,256,512]{4,3,1,0,2:T(8,128)(2,1)}, u32[]{:S(2)}, u32[]{:S(2)}) collective-permute-start(bf16[4,1,2,256,512]{4,3,1,0,2:T(8,128)(2,1)} %get-tuple-element.217), channel_id=1, source_target_pairs={{1,0},{2,1},{3,2},{4,3},{5,4},{6,5},{7,6},{0,7},{9,8},{10,9},{11,1... | collective-permute-start | bytes 6291464 | tf_op jit(solution)/shard_map/ppermute | solution.py:23
  49.8 1.3 copy-start
  139.9 4.7 copy-start.12
  145.5 1.3 copy-start.13
  153.7 4.7 copy-start.12
  159.3 1.3 copy-start.13
  167.5 4.7 copy-start.12
  173.2 1.3 copy-start.13
  181.4 4.7 copy-start.12
  187.0 1.3 copy-start.13
  200.0 3.6 copy-start.1
  205.6 1.3 copy-start.2
  213.8 3.6 copy-start.1
  219.4 1.3 copy-start.2
  227.6 3.6 copy-start.1
  233.2 1.3 copy-start.2
  241.4 3.6 copy-start.1
  247.0 1.3 copy-start.2
  251.0 11.9 %copy-start.3 = (bf16[4,4,64,8,64]{4,2,3,1,0:T(8,128)(2,1)S(1)}, bf16[4,4,64,8,64]{4,2,3,1,0:T(8,128)(2,1)}, u32[]{:S(2)}) copy-start(bf16[4,4,64,8,64]{4,2,3,1,0:T(8,128)(2,1)} %get-tuple-element.134) | copy-start | bytes 3145732
  253.1 19.3 %collective-permute-start.4 = (bf16[1,2,256,512]{3,2,1,0:T(8,128)(2,1)}, bf16[1,2,256,512]{3,2,1,0:T(8,128)(2,1)}, u32[]{:S(2)}, u32[]{:S(2)}) collective-permute-start(bf16[1,2,256,512]{3,2,1,0:T(8,128)(2,1)} %slice.63), channel_id=1, source_target_pairs={{0,8},{8,16},{16,24},{24,32},{32,40},{40,48},{48,56},{56,64},{64,7... | collective-permute-start | bytes 1572872 | tf_op jit(solution)/shard_map/ppermute | solution.py:21
  257.0 17.6 %collective-permute-start.5 = (bf16[1,2,256,512]{3,2,1,0:T(8,128)(2,1)}, bf16[1,2,256,512]{3,2,1,0:T(8,128)(2,1)}, u32[]{:S(2)}, u32[]{:S(2)}) collective-permute-start(bf16[1,2,256,512]{3,2,1,0:T(8,128)(2,1)} %slice.65), channel_id=1, source_target_pairs={{8,0},{16,8},{24,16},{32,24},{40,32},{48,40},{56,48},{64,56},{72,6... | collective-permute-start | bytes 1572872 | tf_op jit(solution)/shard_map/ppermute | solution.py:23
  269.2 9.3 %copy-start.8 = (bf16[2,2,256,512]{3,2,1,0:T(8,128)(2,1)}, bf16[2,2,256,512]{3,2,1,0:T(8,128)(2,1)S(1)}, u32[]{:S(2)}) copy-start(bf16[2,2,256,512]{3,2,1,0:T(8,128)(2,1)S(1)} %convert_element_type.60) | copy-start | bytes 3145732
  269.3 12.4 %copy-start.5 = (bf16[4,4,64,8,64]{4,3,2,1,0:T(8,128)(2,1)S(1)}, bf16[4,4,64,8,64]{4,3,2,1,0:T(8,128)(2,1)}, u32[]{:S(2)}) copy-start(bf16[4,4,64,8,64]{4,3,2,1,0:T(8,128)(2,1)} %copy.28) | copy-start | bytes 3145732
  275.6 1.4 copy-start.7
  278.6 27.2 %collective-permute-start.6 = (bf16[4,1,256,512]{3,2,1,0:T(8,128)(2,1)}, bf16[4,1,256,512]{3,2,1,0:T(8,128)(2,1)}, u32[]{:S(2)}, u32[]{:S(2)}) collective-permute-start(bf16[4,1,256,512]{3,2,1,0:T(8,128)(2,1)} %get-tuple-element.220), channel_id=1, source_target_pairs={{0,1},{1,2},{2,3},{3,4},{4,5},{5,6},{6,7},{7,0},{8,9},{9,10},{10,1... | collective-permute-start | bytes 3145736 | tf_op jit(solution)/shard_map/ppermute | solution.py:21
  278.6 42.8 %collective-permute-start.7 = (bf16[4,1,256,512]{3,2,1,0:T(8,128)(2,1)}, bf16[4,1,256,512]{3,2,1,0:T(8,128)(2,1)}, u32[]{:S(2)}, u32[]{:S(2)}) collective-permute-start(bf16[4,1,256,512]{3,2,1,0:T(8,128)(2,1)} %get-tuple-element.221), channel_id=1, source_target_pairs={{1,0},{2,1},{3,2},{4,3},{5,4},{6,5},{7,6},{0,7},{9,8},{10,9},{11,1... | collective-permute-start | bytes 3145736 | tf_op jit(solution)/shard_map/ppermute | solution.py:23
  394.1 12.0 %copy-start.9 = (bf16[2,2,256,512]{3,2,1,0:T(8,128)(2,1)S(1)}, bf16[2,2,256,512]{3,2,1,0:T(8,128)(2,1)}, u32[]{:S(2)}) copy-start(bf16[2,2,256,512]{3,2,1,0:T(8,128)(2,1)} %copy-done.8) | copy-start | bytes 3145732
  395.1 22.0 %collective-permute-start.8 = (bf16[1,2,256,512]{3,2,1,0:T(8,128)(2,1)}, bf16[1,2,256,512]{3,2,1,0:T(8,128)(2,1)}, u32[]{:S(2)}, u32[]{:S(2)}) collective-permute-start(bf16[1,2,256,512]{3,2,1,0:T(8,128)(2,1)} %bitcast.58), channel_id=1, source_target_pairs={{0,8},{8,16},{16,24},{24,32},{32,40},{40,48},{48,56},{56,64},{64,7... | collective-permute-start | bytes 1572872 | tf_op jit(solution)/shard_map/ppermute | solution.py:21
  395.1 22.0 %collective-permute-start.9 = (bf16[1,2,256,512]{3,2,1,0:T(8,128)(2,1)}, bf16[1,2,256,512]{3,2,1,0:T(8,128)(2,1)}, u32[]{:S(2)}, u32[]{:S(2)}) collective-permute-start(bf16[1,2,256,512]{3,2,1,0:T(8,128)(2,1)} %bitcast.59), channel_id=1, source_target_pairs={{8,0},{16,8},{24,16},{32,24},{40,32},{48,40},{56,48},{64,56},{72,6... | collective-permute-start | bytes 1572872 | tf_op jit(solution)/shard_map/ppermute | solution.py:23
  408.0 15.0 %copy-start.14 = (bf16[1024,512]{1,0:T(8,128)(2,1)S(1)}, bf16[1024,512]{1,0:T(8,128)(2,1)}, u32[]{:S(2)}) copy-start(bf16[1024,512]{1,0:T(8,128)(2,1)} %param.16) | copy-start | bytes 3145732
  420.1 27.2 %collective-permute-start.10 = (bf16[4,1,256,512]{3,2,1,0:T(8,128)(2,1)}, bf16[4,1,256,512]{3,2,1,0:T(8,128)(2,1)}, u32[]{:S(2)}, u32[]{:S(2)}) collective-permute-start(bf16[4,1,256,512]{3,2,1,0:T(8,128)(2,1)} %get-tuple-element.218), channel_id=1, source_target_pairs={{0,1},{1,2},{2,3},{3,4},{4,5},{5,6},{6,7},{7,0},{8,9},{9,10},{10,1... | collective-permute-start | bytes 3145736 | tf_op jit(solution)/shard_map/ppermute | solution.py:21
  420.1 39.5 %collective-permute-start.11 = (bf16[4,1,256,512]{3,2,1,0:T(8,128)(2,1)}, bf16[4,1,256,512]{3,2,1,0:T(8,128)(2,1)}, u32[]{:S(2)}, u32[]{:S(2)}) collective-permute-start(bf16[4,1,256,512]{3,2,1,0:T(8,128)(2,1)} %get-tuple-element.219), channel_id=1, source_target_pairs={{1,0},{2,1},{3,2},{4,3},{5,4},{6,5},{7,6},{0,7},{9,8},{10,9},{11,1... | collective-permute-start | bytes 3145736 | tf_op jit(solution)/shard_map/ppermute | solution.py:23
where the time goes:
time: 531 us; the launch traced here: 525 us
  local copies, waits for them, and re-layouts  197 us (37%)
  waiting for transfers between devices  180 us (34%)
  matrix products  83 us (16%)
  other arithmetic  34.1 us (6%)
  starting transfers between devices  30.2 us (6%)
    ppermute x6, waiting for transfers between devices, extended_2(): lax.ppermute(tail, axis, [(i, (i + 1) % count) for i in range(count)])  108 us
    ppermute x6, waiting for transfers between devices, extended_2(): lax.ppermute(head, axis, [((i + 1) % count, i) for i in range(count)])  72.3 us
    reshape x16, local copies, waits for them, and re-layouts, product_rows(): far_rows = extended[place_rows].reshape(group, NB, BS, NB, BS)  57.6 us
    dot_general x16, matrix products, product_rows(): jnp.einsum('iasct,iacb->iasbt', far_rows, map_rows, preferred_element_typ...  55.8 us
    gather x16, local copies, waits for them, and re-layouts, product_rows(): far_rows = extended[place_rows].reshape(group, NB, BS, NB, BS)  50.7 us
    ppermute x6, starting transfers between devices, extended_2(): lax.ppermute(head, axis, [((i + 1) % count, i) for i in range(count)])  28 us
    dot_general x16, matrix products, product_rows(): jnp.einsum('iras,iasbt->irbt', left_rows, moved, preferred_element_type=j...  27.1 us
    mul x3, local copies, waits for them, and re-layouts, body(): 2.0 * fifth  14.8 us
  transfers between devices with their start and end apart: 12, of which 11 were waited for; matrix products, arithmetic and copies ran while one was open for 6% of the time, Pallas kernels for 0%

commit v1 on v0

v1 whole, which is shorter than its diff:
```python
import functools

import jax
import jax.numpy as jnp
from jax import lax
from jax.experimental import pallas as pl
from jax.experimental.pallas import tpu as pltpu
from jax.sharding import PartitionSpec as P

BS = 64
NB = 8
EDGE = 4
BLK_DEV = 16
AXES = ("gx", "gy")

DIRECTIONS = [(-1, -1), (-1, 0), (-1, 1), (0, -1), (0, 1), (1, -1), (1, 0), (1, 1)]


def sides(step):
    return {-1: (1,), 1: (0,), 0: (0, 1)}[step]


def ghost_clusters(s, t):
    return [EDGE * (2 * p + q) + r for p in sides(s) for q in sides(t) for r in range(EDGE)]


def piece_of(cells, s, t):
    quads = cells.reshape(2, 2, EDGE, BS, NB * BS)
    ps, qs = sides(s), sides(t)
    part = quads[ps[0] : ps[-1] + 1, qs[0] : qs[-1] + 1]
    return part.reshape(-1, BS, NB * BS)


def exchange(cells, nx, ny):
    pieces = [cells]
    for s, t in DIRECTIONS:
        perm = []
        for x in range(nx):
            for y in range(ny):
                perm.append((x * ny + y, ((x - s) % nx) * ny + (y - t) % ny))
        pieces.append(lax.ppermute(piece_of(cells, s, t), AXES, perm))
    return jnp.concatenate(pieces, axis=0)


def product_kernel(mode, pos_ref, tile_ref, swap_ref, live_ref, x_ref, y_ref, *rest):
    if mode == "purify":
        c_ref, o_ref, rhs_ref = rest
    else:
        o_ref, rhs_ref = rest
    rows = x_ref.shape[0]
    low = lax.broadcasted_iota(jnp.int32, (BS, 128), 1) < BS

    def row(i, carry):
        for a in range(NB):
            k = pos_ref[i * NB + a]
            for j in range(NB // 2):
                halves = []
                for h in range(2):
                    idx = (i * NB + a) * NB + 2 * j + h
                    start = pl.multiple_of(tile_ref[idx] * 128, 128)
                    t = y_ref[k, :, pl.ds(start, 128)]
                    t = jnp.where(swap_ref[idx] == 1, pltpu.roll(t, BS, 1), t)
                    t = jnp.where(live_ref[idx] == 1, t, jnp.zeros_like(t))
                    halves.append(t)
                rhs_ref[a * BS : (a + 1) * BS, j * 128 : (j + 1) * 128] = jnp.where(
                    low, halves[0], halves[1]
                )
        acc = jnp.dot(x_ref[i], rhs_ref[...], preferred_element_type=jnp.float32)
        if mode == "purify":
            acc = 3.0 * c_ref[i].astype(jnp.float32) - 2.0 * acc
        o_ref[i] = acc.astype(o_ref.dtype)
        return carry

    lax.fori_loop(0, rows, row, 0)


def pattern_product(tables, left, extended, out_dtype, mode="plain", cubic=None):
    rows = left.shape[0]
    operands = [left, extended] + ([cubic] if mode == "purify" else [])
    vmem = pl.BlockSpec(memory_space=pltpu.VMEM)
    flops = 2 * rows * BS * (NB * BS) ** 2
    nbytes = sum(o.size * o.dtype.itemsize for o in operands) + rows * BS * NB * BS * 4
    return pl.pallas_call(
        functools.partial(product_kernel, mode),
        out_shape=jax.ShapeDtypeStruct(left.shape, out_dtype),
        grid_spec=pltpu.PrefetchScalarGridSpec(
            num_scalar_prefetch=4,
            grid=(),
            in_specs=[vmem] * len(operands),
            out_specs=vmem,
            scratch_shapes=[pltpu.VMEM((NB * BS, NB * BS), jnp.bfloat16)],
        ),
        compiler_params=pltpu.CompilerParams(vmem_limit_bytes=48 * 1024 * 1024),
        cost_estimate=pl.CostEstimate(flops=flops, bytes_accessed=nbytes, transcendentals=0),
    )(*tables, *operands)


def build_tables(columns, nx, ny):
    gx = lax.axis_index("gx")
    gy = lax.axis_index("gy")
    first = (gx * ny + gy) * BLK_DEV
    own = lax.dynamic_slice_in_dim(columns, first, BLK_DEV, 0)
    ids = [first + jnp.arange(BLK_DEV, dtype=jnp.int32)]
    for s, t in DIRECTIONS:
        owner = ((gx + s) % nx) * ny + (gy + t) % ny
        ids.append(owner * BLK_DEV + jnp.array(ghost_clusters(s, t), jnp.int32))
    ext_ids = jnp.concatenate(ids)
    count = ext_ids.shape[0]
    ext_columns = columns[ext_ids]
    live = own >= 0
    found = ext_ids[None, None, :] == own[:, :, None]
    pos = jnp.min(jnp.where(found, jnp.arange(count, dtype=jnp.int32), count), axis=2)
    ok = live & (pos < count)
    pos = jnp.where(ok, pos, 0)
    far = ext_columns[pos]
    matched = (far[:, :, :, None] == own[:, None, None, :]) & ok[:, :, None, None] & live[:, None, None, :]
    slot = jnp.sum(jnp.where(matched, jnp.arange(NB, dtype=jnp.int32)[None, None, :, None], 0), axis=2)
    hit = jnp.any(matched, axis=2)
    b_half = jnp.arange(NB, dtype=jnp.int32)[None, None, :] % 2
    tile = slot // 2
    swap = (slot % 2 != b_half).astype(jnp.int32)
    return (
        pos.reshape(-1),
        tile.reshape(-1),
        swap.reshape(-1),
        hit.astype(jnp.int32).reshape(-1),
    )


def body(kernel, margin, hamiltonian, columns):
    nx = lax.axis_size("gx")
    ny = lax.axis_size("gy")
    tables = build_tables(columns, nx, ny)
    kernel = kernel.reshape(BLK_DEV, BS, NB * BS)
    margin = margin.reshape(BLK_DEV, BS, NB * BS)
    hamiltonian = hamiltonian.reshape(BLK_DEV, BS, NB * BS)
    margin_ext = exchange(margin, nx, ny)
    kernel_ext = exchange(kernel, nx, ny)
    lead = pattern_product(tables, kernel, margin_ext, jnp.bfloat16)
    cubic = pattern_product(tables, lead, kernel_ext, jnp.bfloat16)
    cubic_ext = exchange(cubic, nx, ny)
    purified = pattern_product(tables, lead, cubic_ext, jnp.bfloat16, "purify", cubic)
    purified_ext = exchange(purified, nx, ny)
    out = pattern_product(tables, hamiltonian, purified_ext, jnp.float32)
    return out.reshape(BLK_DEV * BS, NB * BS)


def solution(mesh):
    in_specs = (P(AXES, None), P(AXES, None), P(AXES, None), P())
    out_specs = P(AXES, None)
    return jax.shard_map(body, mesh=mesh, in_specs=in_specs, out_specs=out_specs, check_vma=False)
```

time: 531 us -> 313 us (0.59)
  the two profiles are of different devices: /device:TPU:2 before, /device:TPU:184 now
where the time goes in v1:
time: 313 us
  waiting for transfers between devices  156 us (50%)
  starting transfers between devices  64.7 us (21%)
  Pallas kernels  51.6 us (16%)
  local copies, waits for them, and re-layouts  37.5 us (12%)
    ppermute x32, waiting for transfers between devices, exchange(): pieces.append(lax.ppermute(piece_of(cells, s, t), AXES, perm))  156 us
    ppermute x32, starting transfers between devices, exchange(): pieces.append(lax.ppermute(piece_of(cells, s, t), AXES, perm))  64.7 us
    pallas_call x4, Pallas kernels, pattern_product(): pl.pallas_call(functools.partial(product_kernel, mode), out_shape=jax.Sha...  51.6 us
    unnamed x57, local copies, waits for them, and re-layouts  20.7 us
  transfers between devices with their start and end apart: 32, of which 15 were waited for; matrix products, arithmetic and copies ran while one was open for 11% of the time, Pallas kernels for 4%

profile of v1, /device:TPU:184, one launch (start us, length us, event | category | flops | bytes accessed | tf_op | source)
XLA Modules:
  0.0 312.9 jit_solution(7002506338257565010)
XLA Ops:
  0.0 2.3 slice_bitcast_fusion.12
  2.4 1.5 collective-permute-start
  3.8 2.3 fusion.21
  7.1 1.1 fusion.22
  8.1 2.8 collective-permute-start.3
  11.0 1.0 slice_bitcast_fusion.8
  12.0 1.1 collective-permute-start.8
  13.1 2.8 copy.27
  16.0 0.7 constant_dynamic-slice_fusion
  17.2 0.7 compare_and_fusion
  17.9 0.6 compare_select_fusion
  19.2 1.0 fusion.19
  20.2 1.1 fusion.20
  21.4 2.2 gather_fusion
  23.7 0.6 gather_fusion.1
  25.5 1.1 constant_dynamic-update-slice_fusion.8
  26.6 1.1 constant_dynamic-update-slice_fusion.17
  28.0 0.8 reshape.496.pos_ref
  28.8 1.8 collective-permute-start.4
  30.6 1.7 constant_dynamic-update-slice_fusion.7
  32.3 1.6 collective-permute-done.8
  33.8 10.6 %collective-permute-start.9 = (bf16[8,64,512]{2,1,0:T(8,128)(2,1)}, bf16[8,64,512]{2,1,0:T(8,128)(2,1)S(1)}, u32[]{:S(2)}, u32[]{:S(2)}) collective-permute-start(bf16[8,64,512]{2,1,0:T(8,128)(2,1)} %bitcast.90), channel_id=1, source_target_pairs={{0,8},{1,9},{2,10},{3,11},{4,12},{5,13},{6,14},{7,15},{8,16},{9,17... | collective-permute-start | bytes 1572872 | tf_op jit(solution)/shard_map/ppermute | solution.py:41
  44.5 1.7 constant_dynamic-update-slice_fusion.16
  46.1 1.8 collective-permute-start.5
  47.9 0.9 constant_dynamic-update-slice_fusion.6
  48.7 0.7 constant_dynamic-update-slice_fusion.5
  49.5 11.5 %collective-permute-start.10 = (bf16[4,64,512]{2,1,0:T(8,128)(2,1)}, bf16[4,64,512]{2,1,0:T(8,128)(2,1)S(1)}, u32[]{:S(2)}, u32[]{:S(2)}) collective-permute-start(bf16[4,64,512]{2,1,0:T(8,128)(2,1)} %get-tuple-element.27), channel_id=1, source_target_pairs={{0,15},{1,8},{2,9},{3,10},{4,11},{5,12},{6,13},{7,14},{8,23},{9,16... | collective-permute-start | bytes 786440 | tf_op jit(solution)/shard_map/ppermute | solution.py:41
  60.9 0.9 constant_dynamic-update-slice_fusion.4
  61.8 8.6 %collective-permute-start.11 = (bf16[8,64,512]{2,1,0:T(8,128)(2,1)}, bf16[8,64,512]{2,1,0:T(8,128)(2,1)S(1)}, u32[]{:S(2)}, u32[]{:S(2)}) collective-permute-start(bf16[8,64,512]{2,1,0:T(8,128)(2,1)} %bitcast.89), channel_id=1, source_target_pairs={{0,1},{1,2},{2,3},{3,4},{4,5},{5,6},{6,7},{7,0},{8,9},{9,10},{10,1... | collective-permute-start | bytes 1572872 | tf_op jit(solution)/shard_map/ppermute | solution.py:41
  70.4 0.9 constant_dynamic-update-slice_fusion.3
  71.3 0.8 constant_dynamic-update-slice_fusion.15
  72.1 18.6 %collective-permute-done.5 = bf16[4,64,512]{2,1,0:T(8,128)(2,1)S(1)} collective-permute-done((bf16[4,64,512]{2,1,0:T(8,128)(2,1)}, bf16[4,64,512]{2,1,0:T(8,128)(2,1)S(1)}, u32[]{:S(2)}, u32[]{:S(2)}) %collective-permute-start.5) | collective-permute-done | bytes 262176 | tf_op jit(solution)/shard_map/ppermute | solution.py:41
  90.7 0.8 constant_dynamic-update-slice_fusion.2
  91.4 0.7 constant_dynamic-update-slice_fusion.14
  92.2 0.9 constant_dynamic-update-slice_fusion.1
  93.1 0.8 constant_dynamic-update-slice_fusion.13
  93.9 23.0 %collective-permute-done.7 = bf16[4,64,512]{2,1,0:T(8,128)(2,1)S(1)} collective-permute-done((bf16[4,64,512]{2,1,0:T(8,128)(2,1)}, bf16[4,64,512]{2,1,0:T(8,128)(2,1)S(1)}, u32[]{:S(2)}, u32[]{:S(2)}) %collective-permute-start.7) | collective-permute-done | bytes 262176 | tf_op jit(solution)/shard_map/ppermute | solution.py:41
  117.0 0.7 constant_dynamic-update-slice_fusion.y_ref
  117.7 0.8 constant_dynamic-update-slice_fusion.12
  118.6 13.2 %shard_map.118.x_ref = bf16[16,64,512]{2,1,0:T(8,128)(2,1)S(1)} custom-call(s32[128]{0:T(128)S(1)} %reshape.496.pos_ref, s32[1024]{0:T(1024)S(1)} %add_select_fusion.1.tile_ref, s32[1024]{0:T(1024)S(1)} %fusion.3.swap_ref, s32[1024]{0:T(1024)S(1)} %reshape.531.live_ref, bf16[16,64,512]{2,1,0:T(8,128)(2,1)S(1)} %bitcast.78, ...), custom_call_target="tpu_custom_call" | custom-call | flops 536870912 | bytes 7340032 | tf_op jit(solution)/shard_map/pallas_call | solution.py:83
  131.7 0.7 constant_dynamic-update-slice_fusion.11
  132.4 0.8 constant_dynamic-update-slice_fusion.10
  133.3 0.7 constant_dynamic-update-slice_fusion.9.y_ref
  134.0 13.2 %shard_map.119.rest_0_ = bf16[16,64,512]{2,1,0:T(8,128)(2,1)S(1)} custom-call(s32[128]{0:T(128)S(1)} %reshape.496.pos_ref, s32[1024]{0:T(1024)S(1)} %add_select_fusion.1.tile_ref, s32[1024]{0:T(1024)S(1)} %fusion.3.swap_ref, s32[1024]{0:T(1024)S(1)} %reshape.531.live_ref, bf16[16,64,512]{2,1,0:T(8,128)(2,1)S(1)} %shard_map.118.x_ref, ...), custom_call_target="tpu_custom_call" | custom-call | flops 536870912 | bytes 7340032 | tf_op jit(solution)/shard_map/pallas_call | solution.py:83
  147.4 16.4 %collective-permute-start.16 = (bf16[4,64,512]{2,1,0:T(8,128)(2,1)S(1)}, bf16[4,64,512]{2,1,0:T(8,128)(2,1)S(1)}, u32[]{:S(2)}, u32[]{:S(2)}) collective-permute-start(bf16[4,64,512]{2,1,0:T(8,128)(2,1)S(1)} %get-tuple-element.20), channel_id=1, source_target_pairs={{0,9},{1,10},{2,11},{3,12},{4,13},{5,14},{6,15},{7,8},{8,17},{9,18... | collective-permute-start | bytes 786440 | tf_op jit(solution)/shard_map/ppermute | solution.py:41
  164.4 0.7 collective-permute-start.19
  165.0 0.8 collective-permute-start.18
  165.8 2.7 collective-permute-start.20
  168.6 2.6 collective-permute-done.16
  171.2 1.2 collective-permute-done.17
  172.4 15.6 %collective-permute-done.18 = bf16[4,64,512]{2,1,0:T(8,128)(2,1)S(1)} collective-permute-done((bf16[4,64,512]{2,1,0:T(8,128)(2,1)S(1)}, bf16[4,64,512]{2,1,0:T(8,128)(2,1)S(1)}, u32[]{:S(2)}, u32[]{:S(2)}) %collective-permute-start.18) | collective-permute-done | bytes 262176 | tf_op jit(solution)/shard_map/ppermute | solution.py:41
  188.1 17.7 %collective-permute-done.20 = bf16[8,64,512]{2,1,0:T(8,128)(2,1)S(1)} collective-permute-done((bf16[8,64,512]{2,1,0:T(8,128)(2,1)S(1)}, bf16[8,64,512]{2,1,0:T(8,128)(2,1)S(1)}, u32[]{:S(2)}, u32[]{:S(2)}) %collective-permute-start.20) | collective-permute-done | bytes 524320 | tf_op jit(solution)/shard_map/ppermute | solution.py:41
  205.9 15.3 %collective-permute-done.21 = bf16[4,64,512]{2,1,0:T(8,128)(2,1)S(1)} collective-permute-done((bf16[4,64,512]{2,1,0:T(8,128)(2,1)S(1)}, bf16[4,64,512]{2,1,0:T(8,128)(2,1)S(1)}, u32[]{:S(2)}, u32[]{:S(2)}) %collective-permute-start.21) | collective-permute-done | bytes 262176 | tf_op jit(solution)/shard_map/ppermute | solution.py:41
  221.2 3.7 %collective-permute-done.23 = bf16[4,64,512]{2,1,0:T(8,128)(2,1)S(1)} collective-permute-done((bf16[4,64,512]{2,1,0:T(8,128)(2,1)S(1)}, bf16[4,64,512]{2,1,0:T(8,128)(2,1)S(1)}, u32[]{:S(2)}, u32[]{:S(2)}) %collective-permute-start.23) | collective-permute-done | bytes 262176 | tf_op jit(solution)/shard_map/ppermute | solution.py:41
  224.9 2.0 copy-done.3
  226.9 13.0 %shard_map.120 = bf16[16,64,512]{2,1,0:T(8,128)(2,1)S(1)} custom-call(s32[128]{0:T(128)S(1)} %reshape.496.pos_ref, s32[1024]{0:T(1024)S(1)} %add_select_fusion.1.tile_ref, s32[1024]{0:T(1024)S(1)} %fusion.3.swap_ref, s32[1024]{0:T(1024)S(1)} %reshape.531.live_ref, bf16[16,64,512]{2,1,0:T(8,128)(2,1)S(1)} %shard_map.118.x_ref, ...), custom_call_target="tpu_custom_call" | custom-call | flops 536870912 | bytes 8388608 | tf_op jit(solution)/shard_map/pallas_call | solution.py:83
  240.8 2.1 collective-permute-start.28
  243.0 5.9 %collective-permute-done.24 = bf16[4,64,512]{2,1,0:T(8,128)(2,1)S(1)} collective-permute-done((bf16[4,64,512]{2,1,0:T(8,128)(2,1)S(1)}, bf16[4,64,512]{2,1,0:T(8,128)(2,1)S(1)}, u32[]{:S(2)}, u32[]{:S(2)}) %collective-permute-start.24) | collective-permute-done | bytes 262176 | tf_op jit(solution)/shard_map/ppermute | solution.py:41
  249.2 2.7 collective-permute-done.25
  251.9 14.8 %collective-permute-done.26 = bf16[4,64,512]{2,1,0:T(8,128)(2,1)S(1)} collective-permute-done((bf16[4,64,512]{2,1,0:T(8,128)(2,1)S(1)}, bf16[4,64,512]{2,1,0:T(8,128)(2,1)S(1)}, u32[]{:S(2)}, u32[]{:S(2)}) %collective-permute-start.26) | collective-permute-done | bytes 262176 | tf_op jit(solution)/shard_map/ppermute | solution.py:41
  266.8 14.7 %collective-permute-done.28 = bf16[8,64,512]{2,1,0:T(8,128)(2,1)S(1)} collective-permute-done((bf16[8,64,512]{2,1,0:T(8,128)(2,1)S(1)}, bf16[8,64,512]{2,1,0:T(8,128)(2,1)S(1)}, u32[]{:S(2)}, u32[]{:S(2)}) %collective-permute-start.28) | collective-permute-done | bytes 524320 | tf_op jit(solution)/shard_map/ppermute | solution.py:41
  281.6 15.1 %collective-permute-done.29 = bf16[4,64,512]{2,1,0:T(8,128)(2,1)S(1)} collective-permute-done((bf16[4,64,512]{2,1,0:T(8,128)(2,1)S(1)}, bf16[4,64,512]{2,1,0:T(8,128)(2,1)S(1)}, u32[]{:S(2)}, u32[]{:S(2)}) %collective-permute-start.29) | collective-permute-done | bytes 262176 | tf_op jit(solution)/shard_map/ppermute | solution.py:41
  296.8 3.8 %collective-permute-done.31 = bf16[4,64,512]{2,1,0:T(8,128)(2,1)S(1)} collective-permute-done((bf16[4,64,512]{2,1,0:T(8,128)(2,1)S(1)}, bf16[4,64,512]{2,1,0:T(8,128)(2,1)S(1)}, u32[]{:S(2)}, u32[]{:S(2)}) %collective-permute-start.31) | collective-permute-done | bytes 262176 | tf_op jit(solution)/shard_map/ppermute | solution.py:41
  300.6 12.3 %shard_map.121 = f32[16,64,512]{2,1,0:T(8,128)} custom-call(s32[128]{0:T(128)S(1)} %reshape.496.pos_ref, s32[1024]{0:T(1024)S(1)} %add_select_fusion.1.tile_ref, s32[1024]{0:T(1024)S(1)} %fusion.3.swap_ref, s32[1024]{0:T(1024)S(1)} %reshape.531.live_ref, bf16[16,64,512]{2,1,0:T(8,128)(2,1)S(1)} %bitcast.81, ...), custom_call_target="tpu_custom_call" | custom-call | flops 536870912 | bytes 7340032 | tf_op jit(solution)/shard_map/pallas_call | solution.py:83
  (114 shorter events, 6.4 us)
Async XLA Ops:
  0.0 7.1 %copy-start.2 = (bf16[1024,512]{1,0:T(8,128)(2,1)S(1)}, bf16[1024,512]{1,0:T(8,128)(2,1)}, u32[]{:S(2)}) copy-start(bf16[1024,512]{1,0:T(8,128)(2,1)} %param.13) | copy-start | bytes 3145732
  0.0 11.0 %copy-start = (bf16[1024,512]{1,0:T(8,128)(2,1)S(1)}, bf16[1024,512]{1,0:T(8,128)(2,1)}, u32[]{:S(2)}) copy-start(bf16[1024,512]{1,0:T(8,128)(2,1)} %param.12) | copy-start | bytes 3145732
  2.3 13.6 %copy-start.7 = (s32[4]{0:T(128)S(1)}, s32[4]{0:T(128)}, u32[]{:S(2)}) copy-start(s32[4]{0:T(128)} %constant.135.clone) | copy-start | bytes 52
  2.3 13.6 %copy-start.6 = (s32[8]{0:T(128)S(1)}, s32[8]{0:T(128)}, u32[]{:S(2)}) copy-start(s32[8]{0:T(128)} %constant.136.clone) | copy-start | bytes 100
  2.4 14.3 %copy-start.10 = (s32[4]{0:T(128)S(1)}, s32[4]{0:T(128)}, u32[]{:S(2)}) copy-start(s32[4]{0:T(128)} %constant.137.clone) | copy-start | bytes 52
  2.4 14.3 %copy-start.11 = (s32[4]{0:T(128)S(1)}, s32[4]{0:T(128)}, u32[]{:S(2)}) copy-start(s32[4]{0:T(128)} %constant.140.clone) | copy-start | bytes 52
  2.4 14.3 %copy-start.8 = (s32[8]{0:T(128)S(1)}, s32[8]{0:T(128)}, u32[]{:S(2)}) copy-start(s32[8]{0:T(128)} %constant.138.clone) | copy-start | bytes 100
  2.4 14.3 %copy-start.9 = (s32[8]{0:T(128)S(1)}, s32[8]{0:T(128)}, u32[]{:S(2)}) copy-start(s32[8]{0:T(128)} %constant.139.clone) | copy-start | bytes 100
  2.4 26.4 %collective-permute-start = (bf16[4,64,512]{2,1,0:T(8,128)(2,1)}, bf16[4,64,512]{2,1,0:T(8,128)(2,1)}, u32[]{:S(2)}, u32[]{:S(2)}) collective-permute-start(bf16[4,64,512]{2,1,0:T(8,128)(2,1)} %get-tuple-element.36), channel_id=1, source_target_pairs={{0,9},{1,10},{2,11},{3,12},{4,13},{5,14},{6,15},{7,8},{8,17},{9,18... | collective-permute-start | bytes 786440 | tf_op jit(solution)/shard_map/ppermute | solution.py:41
  6.1 40.0 %collective-permute-start.1 = (bf16[8,64,512]{2,1,0:T(8,128)(2,1)}, bf16[8,64,512]{2,1,0:T(8,128)(2,1)S(1)}, u32[]{:S(2)}, u32[]{:S(2)}) collective-permute-start(bf16[8,64,512]{2,1,0:T(8,128)(2,1)} %bitcast.16), channel_id=1, source_target_pairs={{0,8},{1,9},{2,10},{3,11},{4,12},{5,13},{6,14},{7,15},{8,16},{9,17... | collective-permute-start | bytes 1572872 | tf_op jit(solution)/shard_map/ppermute | solution.py:41
  6.5 42.3 %collective-permute-start.2 = (bf16[4,64,512]{2,1,0:T(8,128)(2,1)}, bf16[4,64,512]{2,1,0:T(8,128)(2,1)S(1)}, u32[]{:S(2)}, u32[]{:S(2)}) collective-permute-start(bf16[4,64,512]{2,1,0:T(8,128)(2,1)} %get-tuple-element.35), channel_id=1, source_target_pairs={{0,15},{1,8},{2,9},{3,10},{4,11},{5,12},{6,13},{7,14},{8,23},{9,16... | collective-permute-start | bytes 786440 | tf_op jit(solution)/shard_map/ppermute | solution.py:41
  8.1 41.3 %collective-permute-start.3 = (bf16[8,64,512]{2,1,0:T(8,128)(2,1)}, bf16[8,64,512]{2,1,0:T(8,128)(2,1)S(1)}, u32[]{:S(2)}, u32[]{:S(2)}) collective-permute-start(bf16[8,64,512]{2,1,0:T(8,128)(2,1)} %bitcast.18), channel_id=1, source_target_pairs={{0,1},{1,2},{2,3},{3,4},{4,5},{5,6},{6,7},{7,0},{8,9},{9,10},{10,1... | collective-permute-start | bytes 1572872 | tf_op jit(solution)/shard_map/ppermute | solution.py:41
  12.0 21.9 %collective-permute-start.8 = (bf16[4,64,512]{2,1,0:T(8,128)(2,1)}, bf16[4,64,512]{2,1,0:T(8,128)(2,1)}, u32[]{:S(2)}, u32[]{:S(2)}) collective-permute-start(bf16[4,64,512]{2,1,0:T(8,128)(2,1)} %get-tuple-element.28), channel_id=1, source_target_pairs={{0,9},{1,10},{2,11},{3,12},{4,13},{5,14},{6,15},{7,8},{8,17},{9,18... | collective-permute-start | bytes 786440 | tf_op jit(solution)/shard_map/ppermute | solution.py:41
  24.5 0.9 copy-start.4
  25.5 2.2 copy-start.5
  28.8 33.0 %collective-permute-start.4 = (bf16[8,64,512]{2,1,0:T(8,128)(2,1)}, bf16[8,64,512]{2,1,0:T(8,128)(2,1)S(1)}, u32[]{:S(2)}, u32[]{:S(2)}) collective-permute-start(bf16[8,64,512]{2,1,0:T(8,128)(2,1)} %bitcast.86), channel_id=1, source_target_pairs={{0,7},{1,0},{2,1},{3,2},{4,3},{5,4},{6,5},{7,6},{8,15},{9,8},{10,9... | collective-permute-start | bytes 1572872 | tf_op jit(solution)/shard_map/ppermute | solution.py:41
  33.8 37.4 %collective-permute-start.9 = (bf16[8,64,512]{2,1,0:T(8,128)(2,1)}, bf16[8,64,512]{2,1,0:T(8,128)(2,1)S(1)}, u32[]{:S(2)}, u32[]{:S(2)}) collective-permute-start(bf16[8,64,512]{2,1,0:T(8,128)(2,1)} %bitcast.90), channel_id=1, source_target_pairs={{0,8},{1,9},{2,10},{3,11},{4,12},{5,13},{6,14},{7,15},{8,16},{9,17... | collective-permute-start | bytes 1572872 | tf_op jit(solution)/shard_map/ppermute | solution.py:41
  46.1 44.5 %collective-permute-start.5 = (bf16[4,64,512]{2,1,0:T(8,128)(2,1)}, bf16[4,64,512]{2,1,0:T(8,128)(2,1)S(1)}, u32[]{:S(2)}, u32[]{:S(2)}) collective-permute-start(bf16[4,64,512]{2,1,0:T(8,128)(2,1)} %get-tuple-element.34), channel_id=1, source_target_pairs={{0,249},{1,250},{2,251},{3,252},{4,253},{5,254},{6,255},{7,248},{8... | collective-permute-start | bytes 786440 | tf_op jit(solution)/shard_map/ppermute | solution.py:41
  48.7 43.4 %collective-permute-start.6 = (bf16[8,64,512]{2,1,0:T(8,128)(2,1)}, bf16[8,64,512]{2,1,0:T(8,128)(2,1)S(1)}, u32[]{:S(2)}, u32[]{:S(2)}) collective-permute-start(bf16[8,64,512]{2,1,0:T(8,128)(2,1)} %bitcast.85), channel_id=1, source_target_pairs={{0,248},{1,249},{2,250},{3,251},{4,252},{5,253},{6,254},{7,255},{8... | collective-permute-start | bytes 1572872 | tf_op jit(solution)/shard_map/ppermute | solution.py:41
  49.5 42.0 %collective-permute-start.10 = (bf16[4,64,512]{2,1,0:T(8,128)(2,1)}, bf16[4,64,512]{2,1,0:T(8,128)(2,1)S(1)}, u32[]{:S(2)}, u32[]{:S(2)}) collective-permute-start(bf16[4,64,512]{2,1,0:T(8,128)(2,1)} %get-tuple-element.27), channel_id=1, source_target_pairs={{0,15},{1,8},{2,9},{3,10},{4,11},{5,12},{6,13},{7,14},{8,23},{9,16... | collective-permute-start | bytes 786440 | tf_op jit(solution)/shard_map/ppermute | solution.py:41
  61.8 31.3 %collective-permute-start.11 = (bf16[8,64,512]{2,1,0:T(8,128)(2,1)}, bf16[8,64,512]{2,1,0:T(8,128)(2,1)S(1)}, u32[]{:S(2)}, u32[]{:S(2)}) collective-permute-start(bf16[8,64,512]{2,1,0:T(8,128)(2,1)} %bitcast.89), channel_id=1, source_target_pairs={{0,1},{1,2},{2,3},{3,4},{4,5},{5,6},{6,7},{7,0},{8,9},{9,10},{10,1... | collective-permute-start | bytes 1572872 | tf_op jit(solution)/shard_map/ppermute | solution.py:41
  71.3 45.7 %collective-permute-start.7 = (bf16[4,64,512]{2,1,0:T(8,128)(2,1)}, bf16[4,64,512]{2,1,0:T(8,128)(2,1)S(1)}, u32[]{:S(2)}, u32[]{:S(2)}) collective-permute-start(bf16[4,64,512]{2,1,0:T(8,128)(2,1)} %get-tuple-element.33), channel_id=1, source_target_pairs={{0,255},{1,248},{2,249},{3,250},{4,251},{5,252},{6,253},{7,254},{8... | collective-permute-start | bytes 786440 | tf_op jit(solution)/shard_map/ppermute | solution.py:41
  90.7 27.1 %collective-permute-start.12 = (bf16[8,64,512]{2,1,0:T(8,128)(2,1)}, bf16[8,64,512]{2,1,0:T(8,128)(2,1)S(1)}, u32[]{:S(2)}, u32[]{:S(2)}) collective-permute-start(bf16[8,64,512]{2,1,0:T(8,128)(2,1)} %bitcast.88), channel_id=1, source_target_pairs={{0,7},{1,0},{2,1},{3,2},{4,3},{5,4},{6,5},{7,6},{8,15},{9,8},{10,9... | collective-permute-start | bytes 1572872 | tf_op jit(solution)/shard_map/ppermute | solution.py:41
  91.4 40.3 %collective-permute-start.13 = (bf16[4,64,512]{2,1,0:T(8,128)(2,1)}, bf16[4,64,512]{2,1,0:T(8,128)(2,1)S(1)}, u32[]{:S(2)}, u32[]{:S(2)}) collective-permute-start(bf16[4,64,512]{2,1,0:T(8,128)(2,1)} %get-tuple-element.26), channel_id=1, source_target_pairs={{0,249},{1,250},{2,251},{3,252},{4,253},{5,254},{6,255},{7,248},{8... | collective-permute-start | bytes 786440 | tf_op jit(solution)/shard_map/ppermute | solution.py:41
  92.2 40.3 %collective-permute-start.14 = (bf16[8,64,512]{2,1,0:T(8,128)(2,1)}, bf16[8,64,512]{2,1,0:T(8,128)(2,1)S(1)}, u32[]{:S(2)}, u32[]{:S(2)}) collective-permute-start(bf16[8,64,512]{2,1,0:T(8,128)(2,1)} %bitcast.87), channel_id=1, source_target_pairs={{0,248},{1,249},{2,250},{3,251},{4,252},{5,253},{6,254},{7,255},{8... | collective-permute-start | bytes 1572872 | tf_op jit(solution)/shard_map/ppermute | solution.py:41
  93.1 40.2 %collective-permute-start.15 = (bf16[4,64,512]{2,1,0:T(8,128)(2,1)}, bf16[4,64,512]{2,1,0:T(8,128)(2,1)S(1)}, u32[]{:S(2)}, u32[]{:S(2)}) collective-permute-start(bf16[4,64,512]{2,1,0:T(8,128)(2,1)} %get-tuple-element.25), channel_id=1, source_target_pairs={{0,255},{1,248},{2,249},{3,250},{4,251},{5,252},{6,253},{7,254},{8... | collective-permute-start | bytes 786440 | tf_op jit(solution)/shard_map/ppermute | solution.py:41
  147.4 23.8 %collective-permute-start.16 = (bf16[4,64,512]{2,1,0:T(8,128)(2,1)S(1)}, bf16[4,64,512]{2,1,0:T(8,128)(2,1)S(1)}, u32[]{:S(2)}, u32[]{:S(2)}) collective-permute-start(bf16[4,64,512]{2,1,0:T(8,128)(2,1)S(1)} %get-tuple-element.20), channel_id=1, source_target_pairs={{0,9},{1,10},{2,11},{3,12},{4,13},{5,14},{6,15},{7,8},{8,17},{9,18... | collective-permute-start | bytes 786440 | tf_op jit(solution)/shard_map/ppermute | solution.py:41
  163.8 8.6 %collective-permute-start.17 = (bf16[8,64,512]{2,1,0:T(8,128)(2,1)S(1)}, bf16[8,64,512]{2,1,0:T(8,128)(2,1)S(1)}, u32[]{:S(2)}, u32[]{:S(2)}) collective-permute-start(bf16[8,64,512]{2,1,0:T(8,128)(2,1)S(1)} %get-tuple-element.22), channel_id=1, source_target_pairs={{0,8},{1,9},{2,10},{3,11},{4,12},{5,13},{6,14},{7,15},{8,16},{9,17... | collective-permute-start | bytes 1572872 | tf_op jit(solution)/shard_map/ppermute | solution.py:41
  164.4 23.7 %collective-permute-start.19 = (bf16[8,64,512]{2,1,0:T(8,128)(2,1)S(1)}, bf16[8,64,512]{2,1,0:T(8,128)(2,1)S(1)}, u32[]{:S(2)}, u32[]{:S(2)}) collective-permute-start(bf16[8,64,512]{2,1,0:T(8,128)(2,1)S(1)} %bitcast.94), channel_id=1, source_target_pairs={{0,1},{1,2},{2,3},{3,4},{4,5},{5,6},{6,7},{7,0},{8,9},{9,10},{10,1... | collective-permute-start | bytes 1572872 | tf_op jit(solution)/shard_map/ppermute | solution.py:41
  165.0 23.0 %collective-permute-start.18 = (bf16[4,64,512]{2,1,0:T(8,128)(2,1)S(1)}, bf16[4,64,512]{2,1,0:T(8,128)(2,1)S(1)}, u32[]{:S(2)}, u32[]{:S(2)}) collective-permute-start(bf16[4,64,512]{2,1,0:T(8,128)(2,1)S(1)} %get-tuple-element.19), channel_id=1, source_target_pairs={{0,15},{1,8},{2,9},{3,10},{4,11},{5,12},{6,13},{7,14},{8,23},{9,16... | collective-permute-start | bytes 786440 | tf_op jit(solution)/shard_map/ppermute | solution.py:41
  165.8 40.0 %collective-permute-start.20 = (bf16[8,64,512]{2,1,0:T(8,128)(2,1)S(1)}, bf16[8,64,512]{2,1,0:T(8,128)(2,1)S(1)}, u32[]{:S(2)}, u32[]{:S(2)}) collective-permute-start(bf16[8,64,512]{2,1,0:T(8,128)(2,1)S(1)} %bitcast.92), channel_id=1, source_target_pairs={{0,7},{1,0},{2,1},{3,2},{4,3},{5,4},{6,5},{7,6},{8,15},{9,8},{10,9... | collective-permute-start | bytes 1572872 | tf_op jit(solution)/shard_map/ppermute | solution.py:41
  171.2 49.9 %collective-permute-start.21 = (bf16[4,64,512]{2,1,0:T(8,128)(2,1)S(1)}, bf16[4,64,512]{2,1,0:T(8,128)(2,1)S(1)}, u32[]{:S(2)}, u32[]{:S(2)}) collective-permute-start(bf16[4,64,512]{2,1,0:T(8,128)(2,1)S(1)} %get-tuple-element.18), channel_id=1, source_target_pairs={{0,249},{1,250},{2,251},{3,252},{4,253},{5,254},{6,255},{7,248},{8... | collective-permute-start | bytes 786440 | tf_op jit(solution)/shard_map/ppermute | solution.py:41
  172.4 48.8 %collective-permute-start.22 = (bf16[8,64,512]{2,1,0:T(8,128)(2,1)S(1)}, bf16[8,64,512]{2,1,0:T(8,128)(2,1)S(1)}, u32[]{:S(2)}, u32[]{:S(2)}) collective-permute-start(bf16[8,64,512]{2,1,0:T(8,128)(2,1)S(1)} %get-tuple-element.21), channel_id=1, source_target_pairs={{0,248},{1,249},{2,250},{3,251},{4,252},{5,253},{6,254},{7,255},{8... | collective-permute-start | bytes 1572872 | tf_op jit(solution)/shard_map/ppermute | solution.py:41
  188.1 36.8 %collective-permute-start.23 = (bf16[4,64,512]{2,1,0:T(8,128)(2,1)S(1)}, bf16[4,64,512]{2,1,0:T(8,128)(2,1)S(1)}, u32[]{:S(2)}, u32[]{:S(2)}) collective-permute-start(bf16[4,64,512]{2,1,0:T(8,128)(2,1)S(1)} %get-tuple-element.17), channel_id=1, source_target_pairs={{0,255},{1,248},{2,249},{3,250},{4,251},{5,252},{6,253},{7,254},{8... | collective-permute-start | bytes 786440 | tf_op jit(solution)/shard_map/ppermute | solution.py:41
  224.9 2.0 copy-start.3
  240.1 8.7 %collective-permute-start.24 = (bf16[4,64,512]{2,1,0:T(8,128)(2,1)S(1)}, bf16[4,64,512]{2,1,0:T(8,128)(2,1)S(1)}, u32[]{:S(2)}, u32[]{:S(2)}) collective-permute-start(bf16[4,64,512]{2,1,0:T(8,128)(2,1)S(1)} %get-tuple-element.12), channel_id=1, source_target_pairs={{0,9},{1,10},{2,11},{3,12},{4,13},{5,14},{6,15},{7,8},{8,17},{9,18... | collective-permute-start | bytes 786440 | tf_op jit(solution)/shard_map/ppermute | solution.py:41
  240.2 11.7 %collective-permute-start.25 = (bf16[8,64,512]{2,1,0:T(8,128)(2,1)S(1)}, bf16[8,64,512]{2,1,0:T(8,128)(2,1)S(1)}, u32[]{:S(2)}, u32[]{:S(2)}) collective-permute-start(bf16[8,64,512]{2,1,0:T(8,128)(2,1)S(1)} %get-tuple-element.14), channel_id=1, source_target_pairs={{0,8},{1,9},{2,10},{3,11},{4,12},{5,13},{6,14},{7,15},{8,16},{9,17... | collective-permute-start | bytes 1572872 | tf_op jit(solution)/shard_map/ppermute | solution.py:41
  240.6 26.2 %collective-permute-start.27 = (bf16[8,64,512]{2,1,0:T(8,128)(2,1)S(1)}, bf16[8,64,512]{2,1,0:T(8,128)(2,1)S(1)}, u32[]{:S(2)}, u32[]{:S(2)}) collective-permute-start(bf16[8,64,512]{2,1,0:T(8,128)(2,1)S(1)} %bitcast.93), channel_id=1, source_target_pairs={{0,1},{1,2},{2,3},{3,4},{4,5},{5,6},{6,7},{7,0},{8,9},{9,10},{10,1... | collective-permute-start | bytes 1572872 | tf_op jit(solution)/shard_map/ppermute | solution.py:41
  240.7 26.1 %collective-permute-start.26 = (bf16[4,64,512]{2,1,0:T(8,128)(2,1)S(1)}, bf16[4,64,512]{2,1,0:T(8,128)(2,1)S(1)}, u32[]{:S(2)}, u32[]{:S(2)}) collective-permute-start(bf16[4,64,512]{2,1,0:T(8,128)(2,1)S(1)} %get-tuple-element.11), channel_id=1, source_target_pairs={{0,15},{1,8},{2,9},{3,10},{4,11},{5,12},{6,13},{7,14},{8,23},{9,16... | collective-permute-start | bytes 786440 | tf_op jit(solution)/shard_map/ppermute | solution.py:41
  240.8 59.8 %copy-start.1 = (bf16[1024,512]{1,0:T(8,128)(2,1)S(1)}, bf16[1024,512]{1,0:T(8,128)(2,1)}, u32[]{:S(2)}) copy-start(bf16[1024,512]{1,0:T(8,128)(2,1)} %param.14) | copy-start | bytes 3145732
  240.8 40.7 %collective-permute-start.28 = (bf16[8,64,512]{2,1,0:T(8,128)(2,1)S(1)}, bf16[8,64,512]{2,1,0:T(8,128)(2,1)S(1)}, u32[]{:S(2)}, u32[]{:S(2)}) collective-permute-start(bf16[8,64,512]{2,1,0:T(8,128)(2,1)S(1)} %bitcast.91), channel_id=1, source_target_pairs={{0,7},{1,0},{2,1},{3,2},{4,3},{5,4},{6,5},{7,6},{8,15},{9,8},{10,9... | collective-permute-start | bytes 1572872 | tf_op jit(solution)/shard_map/ppermute | solution.py:41
  248.8 47.9 %collective-permute-start.29 = (bf16[4,64,512]{2,1,0:T(8,128)(2,1)S(1)}, bf16[4,64,512]{2,1,0:T(8,128)(2,1)S(1)}, u32[]{:S(2)}, u32[]{:S(2)}) collective-permute-start(bf16[4,64,512]{2,1,0:T(8,128)(2,1)S(1)} %get-tuple-element.10), channel_id=1, source_target_pairs={{0,249},{1,250},{2,251},{3,252},{4,253},{5,254},{6,255},{7,248},{8... | collective-permute-start | bytes 786440 | tf_op jit(solution)/shard_map/ppermute | solution.py:41
  251.9 44.8 %collective-permute-start.30 = (bf16[8,64,512]{2,1,0:T(8,128)(2,1)S(1)}, bf16[8,64,512]{2,1,0:T(8,128)(2,1)S(1)}, u32[]{:S(2)}, u32[]{:S(2)}) collective-permute-start(bf16[8,64,512]{2,1,0:T(8,128)(2,1)S(1)} %get-tuple-element.13), channel_id=1, source_target_pairs={{0,248},{1,249},{2,250},{3,251},{4,252},{5,253},{6,254},{7,255},{8... | collective-permute-start | bytes 1572872 | tf_op jit(solution)/shard_map/ppermute | solution.py:41
  266.7 33.8 %collective-permute-start.31 = (bf16[4,64,512]{2,1,0:T(8,128)(2,1)S(1)}, bf16[4,64,512]{2,1,0:T(8,128)(2,1)S(1)}, u32[]{:S(2)}, u32[]{:S(2)}) collective-permute-start(bf16[4,64,512]{2,1,0:T(8,128)(2,1)S(1)} %get-tuple-element.9), channel_id=1, source_target_pairs={{0,255},{1,248},{2,249},{3,250},{4,251},{5,252},{6,253},{7,254},{8... | collective-permute-start | bytes 786440 | tf_op jit(solution)/shard_map/ppermute | solution.py:41
